TPU v7x, 32 devices: a whole 2x2x4 slice. The times are simulated.
32 devices in a mesh: region: 2 (over y), tile: 4 (over z), corner: 2 (over x), kern: 2 (over core).
Axes of the slice: x: 2, y: 2, z: 4, core: 2. Of those that a mesh axis runs over, the one named last changes fastest.
Arguments:
- tile_mask: bfloat16 [16, 256, 256], P(('region', 'tile')), parts along dimension 0, may hold values from -1 to 1
- master_mask: bfloat16 [8, 256, 256], P(('region', 'tile')), parts along dimension 0, may hold values from -1 to 1
- target: bfloat16 [16, 256, 256], P(('region', 'tile')), parts along dimension 0, may hold values from 0 to 1
- inst_master: int32 [16], P(('region', 'tile')), parts along dimension 0, may hold values from 0 to 3, as said below
- inst_shift: int32 [16, 2], P(('region', 'tile')), parts along dimension 0, may hold values from 0 to 255
- kernels: float32 [2, 12, 2, 32, 32], P('corner'), may hold values from -24 to 24
- kernel_weight: float32 [2, 12], P('corner'), may hold values from 0.05 to 1
- corner_dose: float32 [2], P('corner'), may hold values from 0.6 to 1.6
Outputs:
- tile_grad: float32 [16, 256, 256], P(('region', 'tile')), parts along dimension 0
- master_grad: float32 [8, 256, 256], P(('region', 'tile')), parts along dimension 0
There are 2 independent parts, one for each index of `region`. A program takes and returns all parts, laid end to end along the dimension named above; an argument that names none is the same for every part. Nothing has to cross between parts.
Inputs may be any that keep to these rules, and one draw needn't show every extreme that they name: `inst_master`: each master cell is placed in exactly 2 tiles.
All inputs are finite; a program needn't handle non-finite values.
Results may differ from a plain program's by a relative error of at most 0.0003.
Values may be sent and summed in bfloat16 or wider, within the bound.
No kernel may reach another device: no remote copies, remote signals or barrier semaphores. Data moves between devices by JAX's collectives and lax.ppermute only.
A program may use at most 64 MiB of HBM per device.

v0:
```python
import math
import numpy as np
import jax
import jax.numpy as jnp
from jax import lax
from jax.sharding import PartitionSpec as P

P_SIZE = 256
B = 32
precise = lax.Precision.HIGHEST
steepness = 3.0
threshold = 1.0


def band_tables():
    freq = np.arange(B, dtype=np.int64) - B // 2
    pixel = np.arange(P_SIZE, dtype=np.int64)
    angle = (
        2.0 * math.pi / P_SIZE * np.mod(freq[:, None] * pixel[None, :], P_SIZE).astype(np.float64)
    )
    return (jnp.asarray(np.cos(angle), jnp.float32), jnp.asarray(-np.sin(angle), jnp.float32))


def phase_ramp(shift):
    freq = jnp.arange(B, dtype=jnp.int32) - B // 2
    total = (
        freq[None, :, None] * shift[:, 0][:, None, None]
        + freq[None, None, :] * shift[:, 1][:, None, None]
    )
    angle = 2.0 * math.pi / P_SIZE * jnp.mod(total, P_SIZE).astype(jnp.float32)
    return (jnp.cos(angle), -jnp.sin(angle))


def spectra(masks, cos_tab, sin_tab):
    rows_re = jnp.einsum("bx,nxy->nby", cos_tab, masks, precision=precise)
    rows_im = jnp.einsum("bx,nxy->nby", sin_tab, masks, precision=precise)
    spec_re = jnp.einsum("nby,cy->nbc", rows_re, cos_tab, precision=precise) - jnp.einsum(
        "nby,cy->nbc", rows_im, sin_tab, precision=precise
    )
    spec_im = jnp.einsum("nby,cy->nbc", rows_re, sin_tab, precision=precise) + jnp.einsum(
        "nby,cy->nbc", rows_im, cos_tab, precision=precise
    )
    return (spec_re, spec_im)


def back_pixels(x_re, x_im, cos_tab, sin_tab):
    half_re = jnp.einsum("bx,nbc->nxc", cos_tab, x_re, precision=precise) + jnp.einsum(
        "bx,nbc->nxc", sin_tab, x_im, precision=precise
    )
    half_im = jnp.einsum("bx,nbc->nxc", cos_tab, x_im, precision=precise) - jnp.einsum(
        "bx,nbc->nxc", sin_tab, x_re, precision=precise
    )
    return jnp.einsum("nxc,cy->nxy", half_re, cos_tab, precision=precise) + jnp.einsum(
        "nxc,cy->nxy", half_im, sin_tab, precision=precise
    )


def on_device(
    tile_mask, master_mask, target, inst_master, inst_shift, kernels, kernel_weight, corner_dose
):
    cos_tab, sin_tab = band_tables()
    scale = 1.0 / (P_SIZE * P_SIZE)
    local_tiles = tile_mask.shape[0]
    local_masters = master_mask.shape[0]
    tile_count = lax.axis_size("tile")
    tile_pos = lax.axis_index("tile")
    kern_count = lax.axis_size("kern")
    kern_pos = lax.axis_index("kern")
    per_dev = local_tiles // kern_count
    first = kern_pos * per_dev
    region_tiles = tile_count * local_tiles
    region_masters = tile_count * local_masters
    with jax.named_scope("master_spectra"):
        own_re, own_im = spectra(master_mask.astype(jnp.float32), cos_tab, sin_tab)
        own = jnp.stack([own_re, own_im], axis=1)
        every = lax.all_gather(own, "tile", axis=0, tiled=True)
    with jax.named_scope("tile_spectra"):
        mine_mask = lax.dynamic_slice_in_dim(tile_mask, first, per_dev, 0)
        goal = lax.dynamic_slice_in_dim(target, first, per_dev, 0).astype(jnp.float32)
        mine_master = lax.dynamic_slice_in_dim(inst_master, first, per_dev, 0)
        mine_shift = lax.dynamic_slice_in_dim(inst_shift, first, per_dev, 0)
        tile_re, tile_im = spectra(mine_mask.astype(jnp.float32), cos_tab, sin_tab)
        ph_re, ph_im = phase_ramp(mine_shift)
        pick = (
            mine_master[:, None] == jnp.arange(region_masters, dtype=jnp.int32)[None, :]
        ).astype(jnp.float32)
        sel = jnp.sum(pick[:, :, None, None, None] * every[None], axis=1)
        sel_re = sel[:, 0]
        sel_im = sel[:, 1]
        spec_re = tile_re + (ph_re * sel_re - ph_im * sel_im)
        spec_im = tile_im + (ph_re * sel_im + ph_im * sel_re)
    dose = corner_dose[0]
    h_re = kernels[0, :, 0]
    h_im = kernels[0, :, 1]
    weights = kernel_weight[0]
    with jax.named_scope("forward_fields"):
        x_re = h_re[:, None] * spec_re[None] - h_im[:, None] * spec_im[None]
        x_im = h_re[:, None] * spec_im[None] + h_im[:, None] * spec_re[None]
        half_re = jnp.einsum("bx,knbc->knxc", cos_tab, x_re, precision=precise) + jnp.einsum(
            "bx,knbc->knxc", sin_tab, x_im, precision=precise
        )
        half_im = jnp.einsum("bx,knbc->knxc", cos_tab, x_im, precision=precise) - jnp.einsum(
            "bx,knbc->knxc", sin_tab, x_re, precision=precise
        )
        f_re = (
            jnp.einsum("knxc,cy->knxy", half_re, cos_tab, precision=precise)
            + jnp.einsum("knxc,cy->knxy", half_im, sin_tab, precision=precise)
        ) * scale
        f_im = (
            jnp.einsum("knxc,cy->knxy", half_im, cos_tab, precision=precise)
            - jnp.einsum("knxc,cy->knxy", half_re, sin_tab, precision=precise)
        ) * scale
    with jax.named_scope("resist_sensitivity"):
        intensity = jnp.sum(weights[:, None, None, None] * (f_re * f_re + f_im * f_im), axis=0)
        resist = jax.nn.sigmoid(steepness * (dose * intensity - threshold))
        sens = 2.0 * (resist - goal) * resist * (1.0 - resist) * steepness * dose
    with jax.named_scope("adjoint_spectra"):
        g_re = (2.0 * weights)[:, None, None, None] * sens[None] * f_re
        g_im = (2.0 * weights)[:, None, None, None] * sens[None] * f_im
        mid_re = jnp.einsum("knxy,cy->knxc", g_re, cos_tab, precision=precise) - jnp.einsum(
            "knxy,cy->knxc", g_im, sin_tab, precision=precise
        )
        mid_im = jnp.einsum("knxy,cy->knxc", g_re, sin_tab, precision=precise) + jnp.einsum(
            "knxy,cy->knxc", g_im, cos_tab, precision=precise
        )
        out_re = (
            jnp.einsum("bx,knxc->knbc", cos_tab, mid_re, precision=precise)
            - jnp.einsum("bx,knxc->knbc", sin_tab, mid_im, precision=precise)
        ) * scale
        out_im = (
            jnp.einsum("bx,knxc->knbc", cos_tab, mid_im, precision=precise)
            + jnp.einsum("bx,knxc->knbc", sin_tab, mid_re, precision=precise)
        ) * scale
        grad_re = jnp.sum(h_re[:, None] * out_re + h_im[:, None] * out_im, axis=0)
        grad_im = jnp.sum(h_re[:, None] * out_im - h_im[:, None] * out_re, axis=0)
    with jax.named_scope("gradient_exchange"):
        back_re = ph_re * grad_re + ph_im * grad_im
        back_im = ph_re * grad_im - ph_im * grad_re
        tile_slot = tile_pos * local_tiles + first + jnp.arange(per_dev, dtype=jnp.int32)
        tile_pick = (
            tile_slot[:, None] == jnp.arange(region_tiles, dtype=jnp.int32)[None, :]
        ).astype(jnp.float32)
        own_grad = jnp.stack([grad_re, grad_im], axis=1)
        own_back = jnp.stack([back_re, back_im], axis=1)
        tile_part = jnp.sum(tile_pick[:, :, None, None, None] * own_grad[:, None], axis=0)
        master_part = jnp.sum(pick[:, :, None, None, None] * own_back[:, None], axis=0)
        slots = jnp.concatenate([tile_part, master_part], axis=0)
        summed = lax.psum(slots, ("tile", "corner", "kern"))
        mine_tiles = lax.dynamic_slice_in_dim(summed, tile_pos * local_tiles, local_tiles, 0)
        mine_masters = lax.dynamic_slice_in_dim(
            summed, region_tiles + tile_pos * local_masters, local_masters, 0
        )
    with jax.named_scope("pixel_gradients"):
        tile_grad = back_pixels(mine_tiles[:, 0], mine_tiles[:, 1], cos_tab, sin_tab)
        master_grad = back_pixels(mine_masters[:, 0], mine_masters[:, 1], cos_tab, sin_tab)
    return (tile_grad, master_grad)


def solution(mesh):
    return jax.shard_map(
        on_device,
        mesh=mesh,
        in_specs=(
            P(("region", "tile"), None, None),
            P(("region", "tile"), None, None),
            P(("region", "tile"), None, None),
            P(("region", "tile")),
            P(("region", "tile"), None),
            P("corner", None, None, None, None),
            P("corner", None),
            P("corner"),
        ),
        out_specs=(P(("region", "tile"), None, None), P(("region", "tile"), None, None)),
        check_vma=False,
    )
```

profile of v0, /device:TPU:0, one launch (start us, length us, event | category | flops | bytes accessed | tf_op | source)
XLA Modules:
  0.0 185.2 jit_solution(1260496238623281663)
XLA Ops:
  7.3 1.1 fusion.41
  8.4 1.1 fusion.39
  11.4 1.0 convolution_bitcast_fusion.1
  12.4 1.0 convolution_bitcast_fusion
  16.5 1.3 dynamic_slice.20
  20.4 15.1 %all_gather.3 = f32[4,2,32,32]{3,2,1,0:T(8,128)S(1)} all-gather(f32[1,2,32,32]{3,2,1,0:T(8,128)S(1)} %pad_maximum_fusion.1), channel_id=1, replica_groups=mesh['region'=2,'tile'=4,'corner'=2,'kern'=2] {'tile'}, dimensions={0}, use_global_device_ids=true | all-gather | bytes 40960 | tf_op jit(solution)/shard_map/master_spectra/all_gather | solution.py:76
  35.4 1.3 fusion.75
  38.8 1.1 fusion.77
  42.0 2.7 %fusion.83 = f32[12,256,256]{2,1,0:T(8,128)S(1)} fusion(f32[12,256,32]{1,2,0:T(8,128)S(1)} %fusion.15, f32[32,256,1]{1,0,2:T(8,128)S(1)} %copy-done.6), kind=kOutput, calls=%fused_computation.143 | convolution fusion | flops 301989888 | bytes 3571712 | tf_op jit(solution)/shard_map/forward_fields/knxc,cy->knxy/dot_general | solution.py:106
  44.8 4.3 %fusion.84 = f32[12,256,256]{2,1,0:T(8,128)} fusion(f32[12,256,32]{1,2,0:T(8,128)S(1)} %fusion.14, f32[32,256,1]{1,0,2:T(8,128)S(1)} %copy-done.6), kind=kOutput, calls=%fused_computation.144 | convolution fusion | flops 301989888 | bytes 3571712 | tf_op jit(solution)/shard_map/forward_fields/knxc,cy->knxy/dot_general | solution.py:110
  49.1 2.7 %add_multiply_fusion = f32[12,256,256]{2,1,0:T(8,128)S(1)} fusion(f32[12,256,256]{2,1,0:T(8,128)S(1)} %fusion.83, f32[12,256,32]{1,2,0:T(8,128)S(1)} %fusion.14, f32[32,256,1]{1,0,2:T(8,128)S(1)} %copy-done.5), kind=kOutput, calls=%fused_computation.4 | convolution fusion | flops 303562752 | bytes 6717440 | tf_op jit(solution)/shard_map/forward_fields/knxc,cy->knxy/dot_general | solution.py:107
  52.5 5.6 %multiply_reduce_fusion = (f32[256,256]{1,0:T(8,128)S(1)}, f32[12,256,256]{2,1,0:T(8,128)S(1)}) fusion(f32[12,256,256]{2,1,0:T(8,128)S(1)} %add_multiply_fusion, f32[12]{0:T(128)S(1)} %bitcast.235, f32[12,256,256]{2,1,0:T(8,128)} %fusion.84, f32[12,256,32]{1,2,0:T(8,128)} %copy-done.7, f32[32,256,1]{1,0,2:T(8,128)S(1)} %copy-done.5), kind=kOutput, calls=%fused_computation.2 | convolution fusion | flops 307429376 | bytes 10125360 | tf_op jit(solution)/shard_map/forward_fields/knxc,cy->knxy/dot_general | solution.py:111
  58.3 3.3 %fusion = f32[12,256,32]{1,2,0:T(8,128)S(1)} fusion(f32[32,256,1]{1,0,2:T(8,128)S(1)} %copy-done.5, f32[12,256,256]{2,1,0:T(8,128)S(1)} %add_multiply_fusion, f32[256,256]{1,0:T(8,128)S(1)} %fusion.32, f32[12]{0:T(128)S(1)} %broadcast_multiply_fusion.2), kind=kOutput, calls=%fused_computation.5 | convolution fusion | flops 303562752 | bytes 3833904 | tf_op jit(solution)/shard_map/adjoint_spectra/knxy,cy->knxc/dot_general | solution.py:123
  61.6 3.3 %fusion.1 = f32[12,256,32]{1,2,0:T(8,128)S(1)} fusion(f32[32,256,1]{1,0,2:T(8,128)S(1)} %copy-done.6, f32[12,256,256]{2,1,0:T(8,128)S(1)} %add_multiply_fusion, f32[256,256]{1,0:T(8,128)S(1)} %fusion.32, f32[12]{0:T(128)S(1)} %broadcast_multiply_fusion.2), kind=kOutput, calls=%fused_computation.6 | convolution fusion | flops 303562752 | bytes 3833904 | tf_op jit(solution)/shard_map/adjoint_spectra/knxy,cy->knxc/dot_general | solution.py:120
  64.8 3.3 %fusion.13 = f32[12,256,32]{1,2,0:T(8,128)S(1)} fusion(f32[12,256,32]{1,2,0:T(8,128)S(1)} %fusion, f32[32,256,1]{1,0,2:T(8,128)S(1)} %copy-done.6, f32[12,256,256]{2,1,0:T(8,128)S(1)} %get-tuple-element.11, f32[256,256]{1,0:T(8,128)S(1)} %fusion.32, f32[12]{0:T(128)S(1)} %broadcast_multiply_fusion.2), kind=kOutput, calls=%fused_computation.19 | convolution fusion | flops 303661056 | bytes 4227120 | tf_op jit(solution)/shard_map/adjoint_spectra/knxy,cy->knxc/dot_general | solution.py:123
  68.2 3.5 %fusion.12 = f32[12,256,32]{1,2,0:T(8,128)S(1)} fusion(f32[12,256,32]{1,2,0:T(8,128)S(1)} %fusion.1, f32[32,256,1]{1,0,2:T(8,128)S(1)} %copy-done.5, f32[12,256,256]{2,1,0:T(8,128)S(1)} %get-tuple-element.11, f32[256,256]{1,0:T(8,128)S(1)} %fusion.32, f32[12]{0:T(128)S(1)} %broadcast_multiply_fusion.2), kind=kOutput, calls=%fused_computation.18 | convolution fusion | flops 303661056 | bytes 4227120 | tf_op jit(solution)/shard_map/adjoint_spectra/knxy,cy->knxc/dot_general | solution.py:120
  74.9 91.9 %all-reduce.2.cloned.1.call-done = f32[12,2,32,32]{3,2,1,0:T(8,128)} async-done(((f32[12,2,32,32]{3,2,1,0:T(8,128)}), f32[12,2,32,32]{3,2,1,0:T(8,128)}) %all-reduce.2.cloned.1.call-update) | async-done | bytes 98320 | tf_op jit(solution)/shard_map/gradient_exchange/psum | solution.py:148
  167.8 0.9 fusion.24
  169.2 1.0 fusion.53
  170.2 1.0 fusion.22
  173.7 1.1 fusion.16
  174.9 1.0 fusion.54
  175.9 1.0 fusion.21
  176.9 1.4 convolution_add_fusion
  (67 shorter events, 18.8 us)
Async XLA Ops:
  7.2 4.2 %copy-start = (bf16[2,256,256]{2,1,0:T(8,128)(2,1)S(1)}, bf16[2,256,256]{2,1,0:T(8,128)(2,1)}, u32[]{:S(2)}) copy-start(bf16[2,256,256]{2,1,0:T(8,128)(2,1)} %param.10) | copy-start | bytes 786436
  7.2 33.0 %copy-start.6 = (f32[32,256,1]{1,0,2:T(8,128)S(1)}, f32[32,256,1]{1,0,2:T(8,128)}, u32[]{:S(2)}) copy-start(f32[32,256,1]{1,0,2:T(8,128)} %constant.68) | copy-start | bytes 98308
  7.2 33.9 %copy-start.5 = (f32[32,256,1]{1,0,2:T(8,128)S(1)}, f32[32,256,1]{1,0,2:T(8,128)}, u32[]{:S(2)}) copy-start(f32[32,256,1]{1,0,2:T(8,128)} %constant.69) | copy-start | bytes 98308
  7.2 159.6 %all-reduce.2.cloned.1.call-start = ((), (), s32[]{:S(2)}) async-start(), calls=%async_computation | async-start | bytes 786432 | tf_op jit(solution)/shard_map/gradient_exchange/psum | solution.py:148
  40.0 4.8 %copy-start.1 = (f32[1,12,1,32,32]{3,4,1,2,0:T(8,128)}, f32[1,12,1,32,32]{3,4,1,2,0:T(8,128)S(1)}, u32[]{:S(2)}) copy-start(f32[1,12,1,32,32]{3,4,1,2,0:T(8,128)S(1)} %copy.22) | copy-start | bytes 147460
  40.1 4.6 %copy-start.3 = (f32[1,12,1,32,32]{3,4,1,2,0:T(8,128)}, f32[1,12,1,32,32]{3,4,1,2,0:T(8,128)S(1)}, u32[]{:S(2)}) copy-start(f32[1,12,1,32,32]{3,4,1,2,0:T(8,128)S(1)} %copy.23) | copy-start | bytes 147460
  42.0 2.8 %copy-start.7 = (f32[12,256,32]{1,2,0:T(8,128)}, f32[12,256,32]{1,2,0:T(8,128)S(1)}, u32[]{:S(2)}) copy-start(f32[12,256,32]{1,2,0:T(8,128)S(1)} %fusion.15) | copy-start | bytes 1179652
  49.1 3.4 %copy-start.11 = (f32[1,12]{1,0:T(1,128)S(1)}, f32[1,12]{1,0:T(1,128)}, u32[]{:S(2)}) copy-start(f32[1,12]{1,0:T(1,128)} %param.16) | copy-start | bytes 148
  52.5 5.6 %copy-start.10 = (bf16[2,256,256]{2,1,0:T(8,128)(2,1)S(1)}, bf16[2,256,256]{2,1,0:T(8,128)(2,1)}, u32[]{:S(2)}) copy-start(bf16[2,256,256]{2,1,0:T(8,128)(2,1)} %param.12) | copy-start | bytes 786436
  68.1 4.9 %copy-start.2 = (f32[1,12,1,32,32]{3,4,1,2,0:T(8,128)S(1)}, f32[1,12,1,32,32]{3,4,1,2,0:T(8,128)}, u32[]{:S(2)}) copy-start(f32[1,12,1,32,32]{3,4,1,2,0:T(8,128)} %copy-done.1) | copy-start | bytes 147460
  68.1 4.9 %copy-start.4 = (f32[1,12,1,32,32]{3,4,1,2,0:T(8,128)S(1)}, f32[1,12,1,32,32]{3,4,1,2,0:T(8,128)}, u32[]{:S(2)}) copy-start(f32[1,12,1,32,32]{3,4,1,2,0:T(8,128)} %copy-done.3) | copy-start | bytes 147460
  71.6 95.2 %copy-start.9 = (f32[32,256]{1,0:T(8,128)S(1)}, f32[32,256]{1,0:T(8,128)}, u32[]{:S(2)}) copy-start(f32[32,256]{1,0:T(8,128)} %constant.58.clone) | copy-start | bytes 98308
  71.7 96.1 %copy-start.8 = (f32[32,256]{1,0:T(8,128)S(1)}, f32[32,256]{1,0:T(8,128)}, u32[]{:S(2)}) copy-start(f32[32,256]{1,0:T(8,128)} %constant.59.clone) | copy-start | bytes 98308
Sparse Core Ops, SparseCore 0:
  75.0 91.7 all-reduce.1
where the time goes:
time: 187 us; the launch traced here: 185 us
  waiting for transfers between devices  91.9 us (49%)
  matrix products  55.3 us (30%)
  between operations  15.2 us (8%)
  blocking collectives  15.1 us (8%)
  local copies, waits for them, and re-layouts  4.24 us (2%)
  other arithmetic  3.34 us (2%)
    psum x1, waiting for transfers between devices, on_device(): summed = lax.psum(slots, ('tile', 'corner', 'kern'))  91.9 us
    all_gather x1, blocking collectives, on_device(): every = lax.all_gather(own, 'tile', axis=0, tiled=True)  15.1 us
    dot_general x1, matrix products, on_device(): jnp.einsum('knxc,cy->knxy', half_re, sin_tab, precision=precise)  5.58 us
    dot_general x1, matrix products, on_device(): jnp.einsum('knxc,cy->knxy', half_im, cos_tab, precision=precise)  4.34 us
  transfers between devices with their start and end apart: 1, of which 1 were waited for; matrix products, arithmetic and copies ran while one was open for 0% of the time, Pallas kernels for 0%

commit v1 on v0

--- a/solution.py
+++ b/solution.py
@@ -10,6 +10,24 @@
 precise = lax.Precision.HIGHEST
 steepness = 3.0
 threshold = 1.0
+
+
+def ring_gather(array, axis, dim):
+    ways, here, hop = (lax.axis_size(axis), lax.axis_index(axis), array.shape[dim])
+    shape = [n * ways if d == dim else n for d, n in enumerate(array.shape)]
+    full = lax.dynamic_update_slice_in_dim(
+        jnp.zeros(shape, array.dtype), array, here * hop, axis=dim
+    )
+    going_up = going_down = array
+    for far in range(1, ways // 2 + 1):
+        going_up = lax.ppermute(going_up, axis, [(d, (d + 1) % ways) for d in range(ways)])
+        full = lax.dynamic_update_slice_in_dim(full, going_up, (here - far) % ways * hop, axis=dim)
+        if 2 * far < ways:
+            going_down = lax.ppermute(going_down, axis, [(d, (d - 1) % ways) for d in range(ways)])
+            full = lax.dynamic_update_slice_in_dim(
+                full, going_down, (here + far) % ways * hop, axis=dim
+            )
+    return full
 
 
 def band_tables():
@@ -73,7 +91,7 @@
     with jax.named_scope("master_spectra"):
         own_re, own_im = spectra(master_mask.astype(jnp.float32), cos_tab, sin_tab)
         own = jnp.stack([own_re, own_im], axis=1)
-        every = lax.all_gather(own, "tile", axis=0, tiled=True)
+        every = ring_gather(own, "tile", 0)
     with jax.named_scope("tile_spectra"):
         mine_mask = lax.dynamic_slice_in_dim(tile_mask, first, per_dev, 0)
         goal = lax.dynamic_slice_in_dim(target, first, per_dev, 0).astype(jnp.float32)

time: 187 us -> 175 us (0.936)
  blocking collectives: 15.1 us -> 0 us
  starting transfers between devices: 0.04 us -> 5.26 us
  matrix products: 55.3 us -> 50.3 us
  waiting for transfers between devices: 91.9 us -> 94.6 us
    all_gather x1 -> x0, blocking collectives: 15.1 us -> none  [on_device(): every = lax.all_gather(own, 'tile', axis=0, tiled=True)]
    ppermute x0 -> x3, waiting for transfers between devices: none -> 5.66 us  [the longest x2 5.66 us: ring_gather(): lax.ppermute(going_up, axis, [(d, (d + 1) % ways) for d in range(ways)])]
    ppermute x0 -> x3, starting transfers between devices: none -> 5.22 us  [the longest x2 3.14 us: ring_gather(): lax.ppermute(going_up, axis, [(d, (d + 1) % ways) for d in range(ways)])]
    psum x1, waiting for transfers between devices: 91.9 us -> 88.9 us  [on_device(): summed = lax.psum(slots, ('tile', 'corner', 'kern'))]
    dot_general x1, matrix products: 5.58 us -> 3.6 us  [on_device(): jnp.einsum('knxc,cy->knxy', half_re, sin_tab, precision=precise)]
  transfers between devices with their start and end apart: 1 -> 4, of which waited for: 1 -> 2; matrix products, arithmetic and copies ran while one was open for 0% -> 6% of each run, Pallas kernels for 0% -> 0%
where the time goes in v1:
time: 175 us; the launch traced here: 174 us
  waiting for transfers between devices  94.6 us (54%)
  matrix products  50.3 us (29%)
  between operations  15.3 us (9%)
  starting transfers between devices  5.26 us (3%)
  local copies, waits for them, and re-layouts  4.16 us (2%)
  other arithmetic  3.97 us (2%)
    psum x1, waiting for transfers between devices, on_device(): summed = lax.psum(slots, ('tile', 'corner', 'kern'))  88.9 us
    ppermute x2, waiting for transfers between devices, ring_gather(): lax.ppermute(going_up, axis, [(d, (d + 1) % ways) for d in range(ways)])  5.66 us
    dot_general x1, matrix products, on_device(): jnp.einsum('knxc,cy->knxy', half_re, sin_tab, precision=precise)  3.6 us
  transfers between devices with their start and end apart: 4, of which 2 were waited for; matrix products, arithmetic and copies ran while one was open for 6% of the time, Pallas kernels for 0%

profile of v1, /device:TPU:0, one launch (start us, length us, event | category | flops | bytes accessed | tf_op | source)
XLA Modules:
  0.0 173.6 jit_solution(4019067566712141208)
XLA Ops:
  7.3 1.2 fusion.41
  8.4 1.1 fusion.39
  13.3 3.1 %collective-permute-start = (f32[1,2,32,32]{3,2,1,0:T(8,128)S(1)}, f32[1,2,32,32]{3,2,1,0:T(8,128)S(1)}, u32[]{:S(2)}, u32[]{:S(2)}) collective-permute-start(f32[1,2,32,32]{3,2,1,0:T(8,128)S(1)} %pad_maximum_fusion.1), channel_id=1, source_target_pairs={{0,4},{4,8},{8,12},{12,0},{1,5},{5,9},{9,13},{13,1},{2,6},{6,10},{... | collective-permute-start | bytes 24584 | tf_op jit(solution)/shard_map/master_spectra/ppermute | solution.py:23
  16.4 2.1 %collective-permute-start.1 = (f32[1,2,32,32]{3,2,1,0:T(8,128)S(1)}, f32[1,2,32,32]{3,2,1,0:T(8,128)S(1)}, u32[]{:S(2)}, u32[]{:S(2)}) collective-permute-start(f32[1,2,32,32]{3,2,1,0:T(8,128)S(1)} %pad_maximum_fusion.1), channel_id=1, source_target_pairs={{0,12},{4,0},{8,4},{12,8},{1,13},{5,1},{9,5},{13,9},{2,14},{6,2},{... | collective-permute-start | bytes 24584 | tf_op jit(solution)/shard_map/master_spectra/ppermute | solution.py:26
  19.4 1.0 convolution_bitcast_fusion
  22.2 1.2 dynamic_slice.20
  25.4 1.0 fusion.77
  27.2 1.3 fusion.75
  29.6 5.7 %collective-permute-done.2 = f32[1,2,32,32]{3,2,1,0:T(8,128)S(1)} collective-permute-done((f32[1,2,32,32]{3,2,1,0:T(8,128)S(1)}, f32[1,2,32,32]{3,2,1,0:T(8,128)S(1)}, u32[]{:S(2)}, u32[]{:S(2)}) %collective-permute-start.2) | collective-permute-done | bytes 8224 | tf_op jit(solution)/shard_map/master_spectra/ppermute | solution.py:23
  37.7 2.8 %fusion.83 = f32[12,256,256]{2,1,0:T(8,128)S(1)} fusion(f32[12,256,32]{1,2,0:T(8,128)S(1)} %fusion.15, f32[32,256,1]{1,0,2:T(8,128)S(1)} %copy-done.2), kind=kOutput, calls=%fused_computation.147 | convolution fusion | flops 301989888 | bytes 3571712 | tf_op jit(solution)/shard_map/forward_fields/knxc,cy->knxy/dot_general | solution.py:124
  40.5 2.8 %fusion.84 = f32[12,256,256]{2,1,0:T(8,128)S(1)} fusion(f32[12,256,32]{1,2,0:T(8,128)S(1)} %fusion.14, f32[32,256,1]{1,0,2:T(8,128)S(1)} %copy-done.2), kind=kOutput, calls=%fused_computation.148 | convolution fusion | flops 301989888 | bytes 3571712 | tf_op jit(solution)/shard_map/forward_fields/knxc,cy->knxy/dot_general | solution.py:128
  43.3 2.8 %add_multiply_fusion = f32[12,256,256]{2,1,0:T(8,128)S(1)} fusion(f32[12,256,256]{2,1,0:T(8,128)S(1)} %fusion.83, f32[12,256,32]{1,2,0:T(8,128)S(1)} %fusion.14, f32[32,256,1]{1,0,2:T(8,128)S(1)} %copy-done.1), kind=kOutput, calls=%fused_computation.4 | convolution fusion | flops 303562752 | bytes 6717440 | tf_op jit(solution)/shard_map/forward_fields/knxc,cy->knxy/dot_general | solution.py:125
  46.1 3.6 %multiply_reduce_fusion = (f32[256,256]{1,0:T(8,128)S(1)}, f32[12,256,256]{2,1,0:T(8,128)S(1)}) fusion(f32[12,256,256]{2,1,0:T(8,128)S(1)} %add_multiply_fusion, f32[12]{0:T(128)S(1)} %bitcast.243, f32[12,256,256]{2,1,0:T(8,128)S(1)} %fusion.84, f32[12,256,32]{1,2,0:T(8,128)S(1)} %fusion.15, f32[32,256,1]{1,0,2:T(8,128)S(1)} %copy-done.1), kind=kOutput, calls=%fused_computation.2 | convolution fusion | flops 307429376 | bytes 10125360 | tf_op jit(solution)/shard_map/forward_fields/knxc,cy->knxy/dot_general | solution.py:129
  49.8 3.3 %fusion = f32[12,256,32]{1,2,0:T(8,128)S(1)} fusion(f32[32,256,1]{1,0,2:T(8,128)S(1)} %copy-done.1, f32[12,256,256]{2,1,0:T(8,128)S(1)} %add_multiply_fusion, f32[256,256]{1,0:T(8,128)S(1)} %fusion.32, f32[12]{0:T(128)S(1)} %broadcast_multiply_fusion.2), kind=kOutput, calls=%fused_computation.5 | convolution fusion | flops 303562752 | bytes 3833904 | tf_op jit(solution)/shard_map/adjoint_spectra/knxy,cy->knxc/dot_general | solution.py:141
  53.1 3.3 %fusion.1 = f32[12,256,32]{1,2,0:T(8,128)S(1)} fusion(f32[32,256,1]{1,0,2:T(8,128)S(1)} %copy-done.2, f32[12,256,256]{2,1,0:T(8,128)S(1)} %add_multiply_fusion, f32[256,256]{1,0:T(8,128)S(1)} %fusion.32, f32[12]{0:T(128)S(1)} %broadcast_multiply_fusion.2), kind=kOutput, calls=%fused_computation.6 | convolution fusion | flops 303562752 | bytes 3833904 | tf_op jit(solution)/shard_map/adjoint_spectra/knxy,cy->knxc/dot_general | solution.py:138
  56.4 3.3 %fusion.13 = f32[12,256,32]{1,2,0:T(8,128)S(1)} fusion(f32[12,256,32]{1,2,0:T(8,128)S(1)} %fusion, f32[32,256,1]{1,0,2:T(8,128)S(1)} %copy-done.2, f32[12,256,256]{2,1,0:T(8,128)S(1)} %get-tuple-element.11, f32[256,256]{1,0:T(8,128)S(1)} %fusion.32, f32[12]{0:T(128)S(1)} %broadcast_multiply_fusion.2), kind=kOutput, calls=%fused_computation.19 | convolution fusion | flops 303661056 | bytes 4227120 | tf_op jit(solution)/shard_map/adjoint_spectra/knxy,cy->knxc/dot_general | solution.py:141
  59.7 3.3 %fusion.12 = f32[12,256,32]{1,2,0:T(8,128)S(1)} fusion(f32[12,256,32]{1,2,0:T(8,128)S(1)} %fusion.1, f32[32,256,1]{1,0,2:T(8,128)S(1)} %copy-done.1, f32[12,256,256]{2,1,0:T(8,128)S(1)} %get-tuple-element.11, f32[256,256]{1,0:T(8,128)S(1)} %fusion.32, f32[12]{0:T(128)S(1)} %broadcast_multiply_fusion.2), kind=kOutput, calls=%fused_computation.18 | convolution fusion | flops 303661056 | bytes 4227120 | tf_op jit(solution)/shard_map/adjoint_spectra/knxy,cy->knxc/dot_general | solution.py:138
  66.4 88.9 %all-reduce.2.cloned.1.call-done = f32[12,2,32,32]{3,2,1,0:T(8,128)} async-done(((f32[12,2,32,32]{3,2,1,0:T(8,128)}), f32[12,2,32,32]{3,2,1,0:T(8,128)}) %all-reduce.2.cloned.1.call-update) | async-done | bytes 98320 | tf_op jit(solution)/shard_map/gradient_exchange/psum | solution.py:166
  157.6 1.0 fusion.53
  158.6 1.0 fusion.22
  162.2 1.1 fusion.16
  163.3 1.0 fusion.54
  164.3 1.0 fusion.21
  165.4 1.4 convolution_add_fusion
  (67 shorter events, 20.2 us)
Async XLA Ops:
  7.2 11.3 %copy-start = (bf16[2,256,256]{2,1,0:T(8,128)(2,1)S(1)}, bf16[2,256,256]{2,1,0:T(8,128)(2,1)}, u32[]{:S(2)}) copy-start(bf16[2,256,256]{2,1,0:T(8,128)(2,1)} %param.10) | copy-start | bytes 786436
  7.2 28.4 %copy-start.4 = (f32[32,256]{1,0:T(8,128)S(1)}, f32[32,256]{1,0:T(8,128)}, u32[]{:S(2)}) copy-start(f32[32,256]{1,0:T(8,128)} %constant.89.clone) | copy-start | bytes 98308
  7.2 28.1 %copy-start.3 = (f32[32,256]{1,0:T(8,128)S(1)}, f32[32,256]{1,0:T(8,128)}, u32[]{:S(2)}) copy-start(f32[32,256]{1,0:T(8,128)} %constant.90.clone) | copy-start | bytes 98308
  7.2 28.6 %copy-start.2 = (f32[32,256,1]{1,0,2:T(8,128)S(1)}, f32[32,256,1]{1,0,2:T(8,128)}, u32[]{:S(2)}) copy-start(f32[32,256,1]{1,0,2:T(8,128)} %constant.99) | copy-start | bytes 98308
  7.2 29.5 %copy-start.1 = (f32[32,256,1]{1,0,2:T(8,128)S(1)}, f32[32,256,1]{1,0,2:T(8,128)}, u32[]{:S(2)}) copy-start(f32[32,256,1]{1,0,2:T(8,128)} %constant.100) | copy-start | bytes 98308
  7.2 148.1 %all-reduce.2.cloned.1.call-start = ((), (), s32[]{:S(2)}) async-start(), calls=%async_computation | async-start | bytes 786432 | tf_op jit(solution)/shard_map/gradient_exchange/psum | solution.py:166
  13.3 16.2 %collective-permute-start = (f32[1,2,32,32]{3,2,1,0:T(8,128)S(1)}, f32[1,2,32,32]{3,2,1,0:T(8,128)S(1)}, u32[]{:S(2)}, u32[]{:S(2)}) collective-permute-start(f32[1,2,32,32]{3,2,1,0:T(8,128)S(1)} %pad_maximum_fusion.1), channel_id=1, source_target_pairs={{0,4},{4,8},{8,12},{12,0},{1,5},{5,9},{9,13},{13,1},{2,6},{6,10},{... | collective-permute-start | bytes 24584 | tf_op jit(solution)/shard_map/master_spectra/ppermute | solution.py:23
  16.4 13.2 %collective-permute-start.1 = (f32[1,2,32,32]{3,2,1,0:T(8,128)S(1)}, f32[1,2,32,32]{3,2,1,0:T(8,128)S(1)}, u32[]{:S(2)}, u32[]{:S(2)}) collective-permute-start(f32[1,2,32,32]{3,2,1,0:T(8,128)S(1)} %pad_maximum_fusion.1), channel_id=1, source_target_pairs={{0,12},{4,0},{8,4},{12,8},{1,13},{5,1},{9,5},{13,9},{2,14},{6,2},{... | collective-permute-start | bytes 24584 | tf_op jit(solution)/shard_map/master_spectra/ppermute | solution.py:26
  29.5 5.8 %collective-permute-start.2 = (f32[1,2,32,32]{3,2,1,0:T(8,128)S(1)}, f32[1,2,32,32]{3,2,1,0:T(8,128)S(1)}, u32[]{:S(2)}, u32[]{:S(2)}) collective-permute-start(f32[1,2,32,32]{3,2,1,0:T(8,128)S(1)} %collective-permute-done), channel_id=1, source_target_pairs={{0,4},{4,8},{8,12},{12,0},{1,5},{5,9},{9,13},{13,1},{2,6},{6,10},{... | collective-permute-start | bytes 24584 | tf_op jit(solution)/shard_map/master_spectra/ppermute | solution.py:23
  43.3 2.8 %copy-start.6 = (f32[1,12]{1,0:T(1,128)S(1)}, f32[1,12]{1,0:T(1,128)}, u32[]{:S(2)}) copy-start(f32[1,12]{1,0:T(1,128)} %param.16) | copy-start | bytes 148
  46.0 3.6 %copy-start.5 = (bf16[2,256,256]{2,1,0:T(8,128)(2,1)S(1)}, bf16[2,256,256]{2,1,0:T(8,128)(2,1)}, u32[]{:S(2)}) copy-start(bf16[2,256,256]{2,1,0:T(8,128)(2,1)} %param.12) | copy-start | bytes 786436
Sparse Core Ops, SparseCore 0:
  66.5 88.7 all-reduce.1
